TPU v7x, 32 devices: a whole 2x2x4 slice. The times are simulated.
32 devices in a mesh: dp: 4 (over y, x), seq: 8 (over z, core).
Axes of the slice: x: 2, y: 2, z: 4, core: 2. Of those that a mesh axis runs over, the one named last changes fastest.
Arguments:
- queries: bfloat16 [6144, 2048], P(('dp', 'seq')), may hold values from -16 to 16
- keys: bfloat16 [6144, 2048], P(('dp', 'seq')), may hold values from -16 to 16
- values: bfloat16 [6144, 2048], P(('dp', 'seq')), may hold values from -6 to 6
- out_grad: bfloat16 [6144, 2048], P(('dp', 'seq')), may hold values from -6 to 6
- out_weight: bfloat16 [2048, 2048], P('dp'), may hold values from -0.125 to 0.125
- section_ids: int32 [6144], P(('dp', 'seq')), may hold values from 0 to 95, as said below
- masked: int32 [6144], P(('dp', 'seq')), may hold values from 0 to 1, as said below
Outputs:
- query_grad: bfloat16 [6144, 2048], P(('dp', 'seq'))
- key_grad: bfloat16 [6144, 2048], P(('dp', 'seq'))
- value_grad: bfloat16 [6144, 2048], P(('dp', 'seq'))
- weight_grad: float32 [2048, 2048], P('dp')
Inputs may be any that keep to these rules, and one draw needn't show every extreme that they name: `section_ids`: section numbers never fall along the tokens, are constant over each aligned block of 64 tokens, and no section spans two sequences of 1536 tokens. `masked`: the same for all tokens of a section.
All inputs are finite; a program needn't handle non-finite values.
Results may differ from a plain program's by a relative error of at most 0.015.
Values may be sent and summed in bfloat16 or wider, within the bound.
No kernel may reach another device: no remote copies, remote signals or barrier semaphores. Data moves between devices by JAX's collectives and lax.ppermute only.
A program may use at most 128 MiB of HBM per device.

v0:
```python
import jax
import jax.numpy as jnp
from jax import lax
from jax.sharding import PartitionSpec as P

HEAD_DIM = 128


def local(queries, keys, values, out_grad, out_weight, section_ids, masked):
    score_scale = HEAD_DIM ** (-0.5)
    attn_grad = lax.dot_general(
        out_grad,
        lax.all_gather(out_weight, "dp", axis=0, tiled=True),
        (((1,), (1,)), ((), ())),
        preferred_element_type=jnp.float32,
    ).astype(jnp.bfloat16)
    query_h, key_h, value_h = (
        lax.all_to_all(queries, "seq", split_axis=1, concat_axis=0, tiled=True),
        lax.all_to_all(keys, "seq", split_axis=1, concat_axis=0, tiled=True),
        lax.all_to_all(values, "seq", split_axis=1, concat_axis=0, tiled=True),
    )
    grad_h = lax.all_to_all(attn_grad, "seq", split_axis=1, concat_axis=0, tiled=True)
    n_seq = lax.axis_size("seq")
    code = section_ids * 2 + masked
    code_all = lax.all_to_all(
        jnp.broadcast_to(code[None], (n_seq,) + code.shape), "seq", 0, 0, tiled=True
    ).reshape(-1)
    sec_all = code_all // 2
    flag_all = code_all - 2 * sec_all
    grad_plane = lax.all_gather(out_grad, "dp", axis=0, tiled=True)
    seq_span = query_h.shape[0]
    width_here = query_h.shape[1]
    heads_here = width_here // HEAD_DIM
    block_rows = min(512, seq_span)
    num_blocks = seq_span // block_rows
    keys_head = key_h.reshape(seq_span, heads_here, HEAD_DIM)
    values_head = value_h.reshape(seq_span, heads_here, HEAD_DIM)
    visible_key = flag_all == 0

    def block_step(carried, block_item):
        key_acc, value_acc = carried
        query_blk, grad_blk, sec_blk = block_item
        scores = (
            jnp.einsum("qhd,khd->hqk", query_blk, keys_head, preferred_element_type=jnp.float32)
            * score_scale
        )
        allowed = visible_key[None, :] | (sec_blk[:, None] == sec_all[None, :])
        scores = jnp.where(allowed[None], scores, -1e30)
        row_max = jnp.max(scores, axis=2, keepdims=True)
        exp_scores = jnp.exp(scores - row_max)
        attn_probs = exp_scores / jnp.sum(exp_scores, axis=2, keepdims=True)
        probs_low = attn_probs.astype(jnp.bfloat16)
        out_blk = jnp.einsum(
            "hqk,khd->qhd", probs_low, values_head, preferred_element_type=jnp.float32
        ).astype(jnp.bfloat16)
        row_delta = jnp.sum(grad_blk.astype(jnp.float32) * out_blk.astype(jnp.float32), axis=2)
        prob_grad = jnp.einsum(
            "qhd,khd->hqk", grad_blk, values_head, preferred_element_type=jnp.float32
        )
        score_grad = (attn_probs * (prob_grad - row_delta.T[:, :, None])).astype(jnp.bfloat16)
        query_blk_grad = (
            jnp.einsum("hqk,khd->qhd", score_grad, keys_head, preferred_element_type=jnp.float32)
            * score_scale
        ).astype(jnp.bfloat16)
        key_acc = key_acc + jnp.einsum(
            "hqk,qhd->khd", score_grad, query_blk, preferred_element_type=jnp.float32
        )
        value_acc = value_acc + jnp.einsum(
            "hqk,qhd->khd", probs_low, grad_blk, preferred_element_type=jnp.float32
        )
        return ((key_acc, value_acc), (out_blk, query_blk_grad))

    scan_inputs = (
        query_h.reshape(num_blocks, block_rows, heads_here, HEAD_DIM),
        grad_h.reshape(num_blocks, block_rows, heads_here, HEAD_DIM),
        sec_all.reshape(num_blocks, block_rows),
    )
    zero_acc = jnp.zeros((seq_span, heads_here, HEAD_DIM), jnp.float32)
    (key_acc, value_acc), (out_blocks, query_blocks) = lax.scan(
        block_step, (zero_acc, zero_acc), scan_inputs
    )
    out_head = out_blocks.reshape(seq_span, width_here)
    query_grad_h = query_blocks.reshape(seq_span, width_here)
    key_grad_h = (key_acc * score_scale).astype(jnp.bfloat16).reshape(seq_span, width_here)
    value_grad_h = value_acc.astype(jnp.bfloat16).reshape(seq_span, width_here)
    attn_out, query_grad, key_grad, value_grad = (
        lax.all_to_all(out_head, "seq", split_axis=0, concat_axis=1, tiled=True),
        lax.all_to_all(query_grad_h, "seq", split_axis=0, concat_axis=1, tiled=True),
        lax.all_to_all(key_grad_h, "seq", split_axis=0, concat_axis=1, tiled=True),
        lax.all_to_all(value_grad_h, "seq", split_axis=0, concat_axis=1, tiled=True),
    )
    out_plane = lax.all_to_all(attn_out, "dp", split_axis=1, concat_axis=0, tiled=True)
    weight_grad = lax.psum(
        lax.dot_general(
            out_plane, grad_plane, (((0,), (0,)), ((), ())), preferred_element_type=jnp.float32
        ),
        "seq",
    )
    return (query_grad, key_grad, value_grad, weight_grad)


def solution(mesh):
    placed = (
        P(("dp", "seq"), None),
        P(("dp", "seq"), None),
        P(("dp", "seq"), None),
        P(("dp", "seq"), None),
        P("dp", None),
        P(("dp", "seq")),
        P(("dp", "seq")),
    )
    return jax.shard_map(
        local,
        mesh=mesh,
        in_specs=placed,
        out_specs=(
            P(("dp", "seq"), None),
            P(("dp", "seq"), None),
            P(("dp", "seq"), None),
            P("dp", None),
        ),
        check_vma=False,
    )
```

profile of v0, /device:TPU:0, one launch (start us, length us, event | category | flops | bytes accessed | tf_op | source)
XLA Modules:
  0.0 405.7 jit_solution(10119106563263983084)
XLA Ops:
  9.2 6.4 %all-to-all-start.1 = ((s32[8,1,192]{2,1,0:T(1,128)}), s32[8,1,192]{2,1,0:T(1,128)S(1)}, u32[]{:S(2)}, u32[]{:S(2)}) async-start(s32[8,1,192]{2,1,0:T(1,128)} %broadcast_in_dim.36), calls=%async_computation.1 | async-start | bytes 16384 | tf_op jit(solution)/shard_map/all_to_all | solution.py:25
  15.6 2.1 copy.117
  17.7 3.5 all-to-all-done.1
  21.2 3.6 all-to-all-start.2
  25.7 19.9 %all-to-all-done.2 = bf16[192,8,256]{2,0,1:T(8,128)(2,1)S(1)} async-done(((bf16[192,8,256]{2,0,1:T(8,128)(2,1)}), bf16[192,8,256]{2,0,1:T(8,128)(2,1)S(1)}, u32[]{:S(2)}, u32[]{:S(2)}) %all-to-all-start.2) | async-done | bytes 786464 | tf_op jit(solution)/shard_map/all_to_all | solution.py:19
  45.6 3.5 all-to-all-start.4
  49.2 0.9 copy.118
  50.1 19.9 %all-to-all-done.4 = bf16[192,8,256]{2,0,1:T(8,128)(2,1)S(1)} async-done(((bf16[192,8,256]{2,0,1:T(8,128)(2,1)}), bf16[192,8,256]{2,0,1:T(8,128)(2,1)S(1)}, u32[]{:S(2)}, u32[]{:S(2)}) %all-to-all-start.4) | async-done | bytes 786464 | tf_op jit(solution)/shard_map/all_to_all | solution.py:20
  70.1 3.5 all-to-all-start
  73.6 26.4 %all-gather.3.cloned.1.call-done = bf16[2048,2048]{1,0:T(8,128)(2,1)} async-done(((bf16[512,2048]{1,0:T(8,128)(2,1)}), bf16[2048,2048]{1,0:T(8,128)(2,1)}) %all-gather.3.cloned.1.call-update) | async-done | bytes 8388624 | tf_op jit(solution)/shard_map/all_gather | solution.py:13
  100.1 6.5 %convolution_convert_fusion.1 = bf16[192,2048]{1,0:T(8,128)(2,1)S(1)} fusion(bf16[192,2048]{1,0:T(8,128)(2,1)} %param.12, bf16[2048,2048]{1,0:T(8,128)(2,1)} %all-gather.3.cloned.1.call-done), kind=kOutput, calls=%fused_computation.31 | convolution fusion | flops 1611005952 | bytes 9961472 | tf_op jit(solution)/shard_map/dot_general | solution.py:11
  106.6 0.9 copy.116
  107.6 4.6 %all-to-all-start.3 = ((bf16[192,8,256]{2,0,1:T(8,128)(2,1)}), bf16[192,8,256]{2,0,1:T(8,128)(2,1)}, u32[]{:S(2)}, u32[]{:S(2)}) async-start(bf16[192,8,256]{2,0,1:T(8,128)(2,1)} %bitcast.76), calls=%async_computation.3 | async-start | bytes 1572864 | tf_op jit(solution)/shard_map/all_to_all | solution.py:22
  113.7 1.8 copy.68
  115.7 17.5 %all-to-all-done.3 = bf16[192,8,256]{2,0,1:T(8,128)(2,1)} async-done(((bf16[192,8,256]{2,0,1:T(8,128)(2,1)}), bf16[192,8,256]{2,0,1:T(8,128)(2,1)}, u32[]{:S(2)}, u32[]{:S(2)}) %all-to-all-start.3) | async-done | bytes 786464 | tf_op jit(solution)/shard_map/all_to_all | solution.py:22
  133.2 2.0 reshape.128
  135.2 65.2 %while.17 = (s32[]{:T(128)}, f32[1536,2,128]{0,2,1:T(8,128)}, f32[1536,2,128]{0,2,1:T(8,128)}, bf16[3,512,2,128]{3,2,1,0:T(2,128)(2,1)}, bf16[3,512,2,128]{3,2,1...) while((s32[]{:T(128)}, f32[1536,2,128]{0,2,1:T(8,128)}, ...), condition=%wide.region_4.5_spmd.clone, body=%wide.region_0.4_spmd.clone.sunk | while | flops 2435711488 | bytes 120883744 | solution.py:79
  136.1 5.0 %fusion.54 = (f32[2,512]{1,0:T(2,128)S(1)}, f32[2,512,1536]{2,1,0:T(8,128)}) fusion(pred[512,1536]{1,0:T(8,128)(4,1)S(1)} %compare_or_fusion.2, bf16[1536,2,128]{2,0,1:T(8,128)(2,1)S(1)} %get-tuple-element.300, bf16[1,512,2,128]{3,2,1,0:T(2,128)(2,1)S(1)} %constant_dynamic-slice_fusion.8), kind=kOutput, calls=%fused_computation.53.clone.1 | convolution fusion | flops 408946176 | bytes 8130560 | tf_op jit(solution)/shard_map/while/body/eval_jaxpr/sub | solution.py:50
  141.1 3.8 fusion.55
  145.1 1.1 multiply_reduce_fusion.2
  146.2 1.2 multiply_convert_fusion.3
  147.5 2.1 fusion.58
  149.6 1.3 copy_dynamic-update-slice_fusion.3
  150.9 1.8 fusion.56
  153.4 1.9 fusion.57
  156.2 5.0 %fusion.54 = (f32[2,512]{1,0:T(2,128)S(1)}, f32[2,512,1536]{2,1,0:T(8,128)}) fusion(pred[512,1536]{1,0:T(8,128)(4,1)S(1)} %compare_or_fusion.2, bf16[1536,2,128]{2,0,1:T(8,128)(2,1)S(1)} %get-tuple-element.300, bf16[1,512,2,128]{3,2,1,0:T(2,128)(2,1)S(1)} %constant_dynamic-slice_fusion.8), kind=kOutput, calls=%fused_computation.53.clone.1 | convolution fusion | flops 408946176 | bytes 8130560 | tf_op jit(solution)/shard_map/while/body/eval_jaxpr/sub | solution.py:50
  161.2 3.8 fusion.55
  165.2 1.1 multiply_reduce_fusion.2
  166.3 1.2 multiply_convert_fusion.3
  167.6 2.1 fusion.58
  169.7 1.3 copy_dynamic-update-slice_fusion.3
  171.0 3.3 fusion.56
  174.4 3.5 fusion.57
  178.7 5.0 %fusion.54 = (f32[2,512]{1,0:T(2,128)S(1)}, f32[2,512,1536]{2,1,0:T(8,128)}) fusion(pred[512,1536]{1,0:T(8,128)(4,1)S(1)} %compare_or_fusion.2, bf16[1536,2,128]{2,0,1:T(8,128)(2,1)S(1)} %get-tuple-element.300, bf16[1,512,2,128]{3,2,1,0:T(2,128)(2,1)S(1)} %constant_dynamic-slice_fusion.8), kind=kOutput, calls=%fused_computation.53.clone.1 | convolution fusion | flops 408946176 | bytes 8130560 | tf_op jit(solution)/shard_map/while/body/eval_jaxpr/sub | solution.py:50
  183.7 3.8 fusion.55
  187.8 1.1 multiply_reduce_fusion.2
  188.9 1.2 multiply_convert_fusion.3
  190.1 2.1 fusion.58
  192.3 1.3 copy_dynamic-update-slice_fusion.3
  193.6 3.3 fusion.56
  196.9 3.5 fusion.57
  200.4 3.3 all_to_all.145
  203.7 3.8 all-to-all-start.8
  208.2 1.4 all_to_all.137
  209.6 18.5 %all-to-all-done.8 = bf16[8,192,256]{2,1,0:T(8,128)(2,1)S(1)} async-done(((bf16[8,192,256]{2,1,0:T(8,128)(2,1)}), bf16[8,192,256]{2,1,0:T(8,128)(2,1)S(1)}, u32[]{:S(2)}, u32[]{:S(2)}) %all-to-all-start.8) | async-done | bytes 786464 | tf_op jit(solution)/shard_map/all_to_all | solution.py:87
  228.1 3.5 all-to-all-start.6
  232.6 1.0 copy.77
  233.6 18.9 %all-to-all-done.6 = bf16[8,192,256]{2,1,0:T(8,128)(2,1)S(1)} async-done(((bf16[8,192,256]{2,1,0:T(8,128)(2,1)}), bf16[8,192,256]{2,1,0:T(8,128)(2,1)S(1)}, u32[]{:S(2)}, u32[]{:S(2)}) %all-to-all-start.6) | async-done | bytes 786464 | tf_op jit(solution)/shard_map/all_to_all | solution.py:89
  252.5 3.5 all-to-all-start.9
  256.0 1.5 convert_element_type.35
  258.1 1.4 all_to_all.141
  259.5 7.3 %all-to-all-done.9 = bf16[192,4,512]{2,0,1:T(8,128)(2,1)S(1)} async-done(((bf16[192,4,512]{2,0,1:T(8,128)(2,1)}), bf16[192,4,512]{2,0,1:T(8,128)(2,1)S(1)}, u32[]{:S(2)}, u32[]{:S(2)}) %all-to-all-start.9) | async-done | bytes 786464 | tf_op jit(solution)/shard_map/all_to_all | solution.py:92
  266.8 3.5 all-to-all-start.7
  270.5 5.7 %fusion.20 = f32[512,2048]{1,0:T(8,128)} fusion(bf16[768,512]{1,0:T(8,128)(2,1)S(1)} %bitcast.122, bf16[768,2048]{1,0:T(8,128)(2,1)} %all-gather.5.cloned.1.call-done), kind=kOutput, calls=%fused_computation.54 | convolution fusion | flops 1610612736 | bytes 8126464 | tf_op jit(solution)/shard_map/dot_general | solution.py:94
  276.2 1.1 copy-done.14
  277.3 1.4 all_to_all.133
  278.7 16.3 %all-to-all-done.7 = bf16[8,192,256]{2,1,0:T(8,128)(2,1)S(1)} async-done(((bf16[8,192,256]{2,1,0:T(8,128)(2,1)}), bf16[8,192,256]{2,1,0:T(8,128)(2,1)S(1)}, u32[]{:S(2)}, u32[]{:S(2)}) %all-to-all-start.7) | async-done | bytes 786464 | tf_op jit(solution)/shard_map/all_to_all | solution.py:90
  295.0 3.5 all-to-all-start.5
  298.5 1.0 copy.93
  299.5 1.0 copy.94
  300.5 27.8 %all-to-all-done.5 = bf16[8,192,256]{2,1,0:T(8,128)(2,1)S(1)} async-done(((bf16[8,192,256]{2,1,0:T(8,128)(2,1)}), bf16[8,192,256]{2,1,0:T(8,128)(2,1)S(1)}, u32[]{:S(2)}, u32[]{:S(2)}) %all-to-all-start.5) | async-done | bytes 786464 | tf_op jit(solution)/shard_map/all_to_all | solution.py:88
  328.2 1.0 copy.92
  329.2 65.3 %all-reduce.2.cloned.1.call-done = f32[512,2048]{1,0:T(8,128)} async-done(((f32[512,2048]{1,0:T(8,128)}), f32[512,2048]{1,0:T(8,128)}) %all-reduce.2.cloned.1.call-update) | async-done | bytes 4194320 | tf_op jit(solution)/shard_map/psum | solution.py:93
  394.5 4.7 %copy.149 = f32[512,2048]{1,0:T(8,128)} copy(f32[512,2048]{1,0:T(8,128)} %all-reduce.2.cloned.1.call-done) | data formatting | bytes 8388608
  (130 shorter events, 10.7 us)
Async XLA Ops:
  7.2 17.6 %copy-start.11 = (bf16[192,2048]{1,0:T(8,128)(2,1)S(1)}, bf16[192,2048]{1,0:T(8,128)(2,1)}, u32[]{:S(2)}) copy-start(bf16[192,2048]{1,0:T(8,128)(2,1)} %param.11) | copy-start | bytes 2359300
  7.2 92.9 %all-gather.3.cloned.1.call-start = ((), (), s32[]{:S(2)}) async-start(), calls=%async_computation.10 | async-start | bytes 10485760 | tf_op jit(solution)/shard_map/all_gather | solution.py:13
  9.2 12.0 %all-to-all-start.1 = ((s32[8,1,192]{2,1,0:T(1,128)}), s32[8,1,192]{2,1,0:T(1,128)S(1)}, u32[]{:S(2)}, u32[]{:S(2)}) async-start(s32[8,1,192]{2,1,0:T(1,128)} %broadcast_in_dim.36), calls=%async_computation.1 | async-start | bytes 16384 | tf_op jit(solution)/shard_map/all_to_all | solution.py:25
  15.6 33.6 %copy-start.12 = (bf16[192,2048]{1,0:T(8,128)(2,1)S(1)}, bf16[192,2048]{1,0:T(8,128)(2,1)}, u32[]{:S(2)}) copy-start(bf16[192,2048]{1,0:T(8,128)(2,1)} %param.9) | copy-start | bytes 2359300
  21.2 24.5 %all-to-all-start.2 = ((bf16[192,8,256]{2,0,1:T(8,128)(2,1)}), bf16[192,8,256]{2,0,1:T(8,128)(2,1)S(1)}, u32[]{:S(2)}, u32[]{:S(2)}) async-start(bf16[192,8,256]{2,0,1:T(8,128)(2,1)} %bitcast.77), calls=%async_computation.2 | async-start | bytes 1572864 | tf_op jit(solution)/shard_map/all_to_all | solution.py:19
  45.6 24.4 %all-to-all-start.4 = ((bf16[192,8,256]{2,0,1:T(8,128)(2,1)}), bf16[192,8,256]{2,0,1:T(8,128)(2,1)S(1)}, u32[]{:S(2)}, u32[]{:S(2)}) async-start(bf16[192,8,256]{2,0,1:T(8,128)(2,1)} %bitcast.75), calls=%async_computation.4 | async-start | bytes 1572864 | tf_op jit(solution)/shard_map/all_to_all | solution.py:20
  70.1 37.5 %all-to-all-start = ((bf16[192,8,256]{2,0,1:T(8,128)(2,1)}), bf16[192,8,256]{2,0,1:T(8,128)(2,1)S(1)}, u32[]{:S(2)}, u32[]{:S(2)}) async-start(bf16[192,8,256]{2,0,1:T(8,128)(2,1)} %bitcast.78), calls=%async_computation | async-start | bytes 1572864 | tf_op jit(solution)/shard_map/all_to_all | solution.py:18
  107.6 25.7 %all-to-all-start.3 = ((bf16[192,8,256]{2,0,1:T(8,128)(2,1)}), bf16[192,8,256]{2,0,1:T(8,128)(2,1)}, u32[]{:S(2)}, u32[]{:S(2)}) async-start(bf16[192,8,256]{2,0,1:T(8,128)(2,1)} %bitcast.76), calls=%async_computation.3 | async-start | bytes 1572864 | tf_op jit(solution)/shard_map/all_to_all | solution.py:22
  112.2 158.3 %all-gather.5.cloned.1.call-start = ((), (), s32[]{:S(2)}) async-start(), calls=%async_computation.11 | async-start | bytes 3932160 | tf_op jit(solution)/shard_map/all_gather | solution.py:30
  135.2 5.8 %copy-start.3 = (bf16[1536,2,128]{2,0,1:T(8,128)(2,1)}, bf16[1536,2,128]{2,0,1:T(8,128)(2,1)S(1)}, u32[]{:S(2)}) copy-start(bf16[1536,2,128]{2,0,1:T(8,128)(2,1)S(1)} %get-tuple-element.300) | copy-start | bytes 2359300 | tf_op jit(solution)/shard_map/while
  135.3 5.8 %copy-start.7 = (bf16[3,512,2,128]{3,2,1,0:T(2,128)(2,1)}, bf16[3,512,2,128]{3,2,1,0:T(2,128)(2,1)S(1)}, u32[]{:S(2)}) copy-start(bf16[3,512,2,128]{3,2,1,0:T(2,128)(2,1)S(1)} %get-tuple-element.296) | copy-start | bytes 2359300 | tf_op jit(solution)/shard_map/while
  135.3 9.6 %copy-start.9 = (bf16[3,512,2,128]{3,2,1,0:T(2,128)(2,1)}, bf16[3,512,2,128]{3,2,1,0:T(2,128)(2,1)S(1)}, u32[]{:S(2)}) copy-start(bf16[3,512,2,128]{3,2,1,0:T(2,128)(2,1)S(1)} %get-tuple-element.301) | copy-start | bytes 2359300 | tf_op jit(solution)/shard_map/while
  141.1 5.1 %slice-start = ((s8[6291456]{0:T(1024)(128)(4,1)}), s8[4194304]{0:T(1024)(128)(4,1)S(1)}, s32[]{:S(2)}) async-start(s8[6291456]{0:T(1024)(128)(4,1)} %bitcast.119), calls=%async_computation.13 | async-start | bytes 8388608 | tf_op jit(solution)/shard_map/while
  141.1 4.0 copy-start.13
  141.1 5.1 %slice-start.1 = ((s8[6291456]{0:T(1024)(128)(4,1)}), s8[2097152]{0:T(1024)(128)(4,1)S(1)}, s32[]{:S(2)}) async-start(s8[6291456]{0:T(1024)(128)(4,1)} %bitcast.119), calls=%async_computation.14 | async-start | bytes 4194304 | tf_op jit(solution)/shard_map/while
  144.9 2.6 copy-start
  145.1 2.4 copy-start.5
  150.9 2.5 copy-start.1
  150.9 2.5 copy-start.6
  153.4 1.9 copy-start.4
  153.4 1.9 copy-start.8
  153.4 1.9 copy-start.10
  155.3 5.8 %copy-start.3 = (bf16[1536,2,128]{2,0,1:T(8,128)(2,1)}, bf16[1536,2,128]{2,0,1:T(8,128)(2,1)S(1)}, u32[]{:S(2)}) copy-start(bf16[1536,2,128]{2,0,1:T(8,128)(2,1)S(1)} %get-tuple-element.300) | copy-start | bytes 2359300 | tf_op jit(solution)/shard_map/while
  155.3 5.8 %copy-start.7 = (bf16[3,512,2,128]{3,2,1,0:T(2,128)(2,1)}, bf16[3,512,2,128]{3,2,1,0:T(2,128)(2,1)S(1)}, u32[]{:S(2)}) copy-start(bf16[3,512,2,128]{3,2,1,0:T(2,128)(2,1)S(1)} %get-tuple-element.296) | copy-start | bytes 2359300 | tf_op jit(solution)/shard_map/while
  155.3 9.6 %copy-start.9 = (bf16[3,512,2,128]{3,2,1,0:T(2,128)(2,1)}, bf16[3,512,2,128]{3,2,1,0:T(2,128)(2,1)S(1)}, u32[]{:S(2)}) copy-start(bf16[3,512,2,128]{3,2,1,0:T(2,128)(2,1)S(1)} %get-tuple-element.301) | copy-start | bytes 2359300 | tf_op jit(solution)/shard_map/while
  161.2 5.1 %slice-start = ((s8[6291456]{0:T(1024)(128)(4,1)}), s8[4194304]{0:T(1024)(128)(4,1)S(1)}, s32[]{:S(2)}) async-start(s8[6291456]{0:T(1024)(128)(4,1)} %bitcast.119), calls=%async_computation.13 | async-start | bytes 8388608 | tf_op jit(solution)/shard_map/while
  161.2 4.0 copy-start.13
  161.2 5.1 %slice-start.1 = ((s8[6291456]{0:T(1024)(128)(4,1)}), s8[2097152]{0:T(1024)(128)(4,1)S(1)}, s32[]{:S(2)}) async-start(s8[6291456]{0:T(1024)(128)(4,1)} %bitcast.119), calls=%async_computation.14 | async-start | bytes 4194304 | tf_op jit(solution)/shard_map/while
  165.0 2.6 copy-start
  165.2 2.4 copy-start.5
  171.0 3.4 copy-start.1
  171.0 3.4 copy-start.6
  174.4 3.5 copy-start.4
  174.4 3.5 copy-start.8
  174.4 3.5 copy-start.10
  177.9 5.8 %copy-start.3 = (bf16[1536,2,128]{2,0,1:T(8,128)(2,1)}, bf16[1536,2,128]{2,0,1:T(8,128)(2,1)S(1)}, u32[]{:S(2)}) copy-start(bf16[1536,2,128]{2,0,1:T(8,128)(2,1)S(1)} %get-tuple-element.300) | copy-start | bytes 2359300 | tf_op jit(solution)/shard_map/while
  177.9 5.8 %copy-start.7 = (bf16[3,512,2,128]{3,2,1,0:T(2,128)(2,1)}, bf16[3,512,2,128]{3,2,1,0:T(2,128)(2,1)S(1)}, u32[]{:S(2)}) copy-start(bf16[3,512,2,128]{3,2,1,0:T(2,128)(2,1)S(1)} %get-tuple-element.296) | copy-start | bytes 2359300 | tf_op jit(solution)/shard_map/while
  177.9 9.6 %copy-start.9 = (bf16[3,512,2,128]{3,2,1,0:T(2,128)(2,1)}, bf16[3,512,2,128]{3,2,1,0:T(2,128)(2,1)S(1)}, u32[]{:S(2)}) copy-start(bf16[3,512,2,128]{3,2,1,0:T(2,128)(2,1)S(1)} %get-tuple-element.301) | copy-start | bytes 2359300 | tf_op jit(solution)/shard_map/while
  183.7 5.1 %slice-start = ((s8[6291456]{0:T(1024)(128)(4,1)}), s8[4194304]{0:T(1024)(128)(4,1)S(1)}, s32[]{:S(2)}) async-start(s8[6291456]{0:T(1024)(128)(4,1)} %bitcast.119), calls=%async_computation.13 | async-start | bytes 8388608 | tf_op jit(solution)/shard_map/while
  183.7 4.0 copy-start.13
  183.7 5.1 %slice-start.1 = ((s8[6291456]{0:T(1024)(128)(4,1)}), s8[2097152]{0:T(1024)(128)(4,1)S(1)}, s32[]{:S(2)}) async-start(s8[6291456]{0:T(1024)(128)(4,1)} %bitcast.119), calls=%async_computation.14 | async-start | bytes 4194304 | tf_op jit(solution)/shard_map/while
  187.5 2.6 copy-start
  187.7 2.4 copy-start.5
  193.6 3.3 copy-start.1
  193.6 3.3 copy-start.6
  196.9 3.5 copy-start.4
  196.9 3.5 copy-start.8
  196.9 3.5 copy-start.10
  200.4 7.0 %copy-start.2 = (f32[1536,2,128]{0,2,1:T(8,128)S(1)}, f32[1536,2,128]{0,2,1:T(8,128)}, u32[]{:S(2)}) copy-start(f32[1536,2,128]{0,2,1:T(8,128)} %get-tuple-element.70) | copy-start | bytes 4718596
  203.7 24.4 %all-to-all-start.8 = ((bf16[8,192,256]{2,1,0:T(8,128)(2,1)}), bf16[8,192,256]{2,1,0:T(8,128)(2,1)S(1)}, u32[]{:S(2)}, u32[]{:S(2)}) async-start(bf16[8,192,256]{2,1,0:T(8,128)(2,1)} %all_to_all.145), calls=%async_computation.8 | async-start | bytes 1572864 | tf_op jit(solution)/shard_map/all_to_all | solution.py:87
  228.1 24.4 %all-to-all-start.6 = ((bf16[8,192,256]{2,1,0:T(8,128)(2,1)}), bf16[8,192,256]{2,1,0:T(8,128)(2,1)S(1)}, u32[]{:S(2)}, u32[]{:S(2)}) async-start(bf16[8,192,256]{2,1,0:T(8,128)(2,1)} %all_to_all.137), calls=%async_computation.6 | async-start | bytes 1572864 | tf_op jit(solution)/shard_map/all_to_all | solution.py:89
  252.5 14.3 %all-to-all-start.9 = ((bf16[192,4,512]{2,0,1:T(8,128)(2,1)}), bf16[192,4,512]{2,0,1:T(8,128)(2,1)S(1)}, u32[]{:S(2)}, u32[]{:S(2)}) async-start(bf16[192,4,512]{2,0,1:T(8,128)(2,1)} %copy.77), calls=%async_computation.9 | async-start | bytes 1572864 | tf_op jit(solution)/shard_map/all_to_all | solution.py:92
  266.8 28.1 %all-to-all-start.7 = ((bf16[8,192,256]{2,1,0:T(8,128)(2,1)}), bf16[8,192,256]{2,1,0:T(8,128)(2,1)S(1)}, u32[]{:S(2)}, u32[]{:S(2)}) async-start(bf16[8,192,256]{2,1,0:T(8,128)(2,1)} %all_to_all.141), calls=%async_computation.7 | async-start | bytes 1572864 | tf_op jit(solution)/shard_map/all_to_all | solution.py:90
  270.4 124.1 %all-reduce.2.cloned.1.call-start = ((), (), s32[]{:S(2)}) async-start(), calls=%async_computation.12 | async-start | bytes 8388608 | tf_op jit(solution)/shard_map/psum | solution.py:93
  276.2 1.1 copy-start.14
  295.0 33.3 %all-to-all-start.5 = ((bf16[8,192,256]{2,1,0:T(8,128)(2,1)}), bf16[8,192,256]{2,1,0:T(8,128)(2,1)S(1)}, u32[]{:S(2)}, u32[]{:S(2)}) async-start(bf16[8,192,256]{2,1,0:T(8,128)(2,1)} %all_to_all.133), calls=%async_computation.5 | async-start | bytes 1572864 | tf_op jit(solution)/shard_map/all_to_all | solution.py:88
Sparse Core Ops, SparseCore 0:
  9.8 90.1 all-gather.2
  114.8 44.3 all-gather.4
  276.3 118.0 all-reduce.1
where the time goes:
time: 407 us; the launch traced here: 406 us
  waiting for transfers between devices  243 us (60%)
  matrix products  57.8 us (14%)
  starting transfers between devices  39.8 us (10%)
  local copies, waits for them, and re-layouts  35.5 us (9%)
  other arithmetic  15.4 us (4%)
  between operations  14 us (3%)
    psum x1, waiting for transfers between devices, local(): lax.psum(lax.dot_general(out_plane, grad_plane, (((0,), (0,)), ((), ())),...  65.3 us
    all_to_all x1, waiting for transfers between devices, local(): lax.all_to_all(query_grad_h, 'seq', split_axis=0, concat_axis=1, tiled=True)  27.8 us
    all_gather x1, waiting for transfers between devices, local(): lax.all_gather(out_weight, 'dp', axis=0, tiled=True)  26.4 us
    all_to_all x1, waiting for transfers between devices, local(): lax.all_to_all(keys, 'seq', split_axis=1, concat_axis=0, tiled=True)  19.9 us
    all_to_all x1, waiting for transfers between devices, local(): lax.all_to_all(values, 'seq', split_axis=1, concat_axis=0, tiled=True)  19.9 us
    all_to_all x1, waiting for transfers between devices, local(): lax.all_to_all(key_grad_h, 'seq', split_axis=0, concat_axis=1, tiled=True)  18.9 us
    all_to_all x1, waiting for transfers between devices, local(): lax.all_to_all(out_head, 'seq', split_axis=0, concat_axis=1, tiled=True)  18.5 us
    all_to_all x1, waiting for transfers between devices, local(): lax.all_to_all(attn_grad, 'seq', split_axis=1, concat_axis=0, tiled=True)  17.5 us
  transfers between devices with their start and end apart: 13, of which 11 were waited for; matrix products, arithmetic and copies ran while one was open for 23% of the time, Pallas kernels for 0%

commit v1 on v0

--- a/solution.py
+++ b/solution.py
@@ -90,11 +90,14 @@
         lax.all_to_all(value_grad_h, "seq", split_axis=0, concat_axis=1, tiled=True),
     )
     out_plane = lax.all_to_all(attn_out, "dp", split_axis=1, concat_axis=0, tiled=True)
-    weight_grad = lax.psum(
-        lax.dot_general(
-            out_plane, grad_plane, (((0,), (0,)), ((), ())), preferred_element_type=jnp.float32
+    weight_grad = jnp.sum(
+        lax.all_gather(
+            lax.dot_general(
+                out_plane, grad_plane, (((0,), (0,)), ((), ())), preferred_element_type=jnp.float32
+            ),
+            axis_name="seq",
         ),
-        "seq",
+        axis=0,
     )
     return (query_grad, key_grad, value_grad, weight_grad)
 

time: 407 us -> 611 us (1.50)
  waiting for transfers between devices: 243 us -> 383 us
  blocking collectives: 0 us -> 24.4 us
  local copies, waits for them, and re-layouts: 35.5 us -> 58.6 us
  other arithmetic: 15.4 us -> 32.5 us
  matrix products: 57.8 us -> 47.1 us
  starting transfers between devices: 39.8 us -> 49.4 us
    all_gather x0 -> x1, waiting for transfers between devices: none -> 180 us  [local(): lax.all_gather(lax.dot_general(out_plane, grad_plane, (((0,), (0,)), ((),...]
    psum x1 -> x0, waiting for transfers between devices: 65.3 us -> none  [local(): lax.psum(lax.dot_general(out_plane, grad_plane, (((0,), (0,)), ((), ())),...]
    all_to_all x1, waiting for transfers between devices: 16.3 us -> 44.3 us  [local(): lax.all_to_all(value_grad_h, 'seq', split_axis=0, concat_axis=1, tiled=True)]
    all_to_all x0 -> x1, blocking collectives: none -> 24.4 us  [local(): lax.all_to_all(out_head, 'seq', split_axis=0, concat_axis=1, tiled=True)]
    all_to_all x1, waiting for transfers between devices: 19.9 us -> 0.01 us  [local(): lax.all_to_all(values, 'seq', split_axis=1, concat_axis=0, tiled=True)]
    all_to_all x1, waiting for transfers between devices: 0.01 us -> 19.9 us  [local(): lax.all_to_all(queries, 'seq', split_axis=1, concat_axis=0, tiled=True)]
    all_to_all x1 -> x0, waiting for transfers between devices: 18.5 us -> none  [local(): lax.all_to_all(out_head, 'seq', split_axis=0, concat_axis=1, tiled=True)]
    all_to_all x1, waiting for transfers between devices: 18.9 us -> 36.4 us  [local(): lax.all_to_all(key_grad_h, 'seq', split_axis=0, concat_axis=1, tiled=True)]
  transfers between devices with their start and end apart: 13 -> 12, of which waited for: 11 -> 10; matrix products, arithmetic and copies ran while one was open for 23% -> 17% of each run, Pallas kernels for 0% -> 0%
where the time goes in v1:
time: 611 us; the launch traced here: 609 us
  waiting for transfers between devices  383 us (63%)
  local copies, waits for them, and re-layouts  58.6 us (10%)
  starting transfers between devices  49.4 us (8%)
  matrix products  47.1 us (8%)
  other arithmetic  32.5 us (5%)
  blocking collectives  24.4 us (4%)
  between operations  14 us (2%)
    all_gather x1, waiting for transfers between devices, local(): lax.all_gather(lax.dot_general(out_plane, grad_plane, (((0,), (0,)), ((),...  180 us
    all_to_all x1, waiting for transfers between devices, local(): lax.all_to_all(value_grad_h, 'seq', split_axis=0, concat_axis=1, tiled=True)  44.3 us
    all_to_all x1, waiting for transfers between devices, local(): lax.all_to_all(key_grad_h, 'seq', split_axis=0, concat_axis=1, tiled=True)  36.4 us
    all_to_all x1, waiting for transfers between devices, local(): lax.all_to_all(query_grad_h, 'seq', split_axis=0, concat_axis=1, tiled=True)  33.5 us
    all_gather x1, waiting for transfers between devices, local(): lax.all_gather(out_weight, 'dp', axis=0, tiled=True)  26.4 us
    all_to_all x1, blocking collectives, local(): lax.all_to_all(out_head, 'seq', split_axis=0, concat_axis=1, tiled=True)  24.4 us
    all_to_all x1, waiting for transfers between devices, local(): lax.all_to_all(keys, 'seq', split_axis=1, concat_axis=0, tiled=True)  19.9 us
    all_to_all x1, waiting for transfers between devices, local(): lax.all_to_all(queries, 'seq', split_axis=1, concat_axis=0, tiled=True)  19.9 us
  transfers between devices with their start and end apart: 12, of which 10 were waited for; matrix products, arithmetic and copies ran while one was open for 17% of the time, Pallas kernels for 0%

profile of v1, /device:TPU:0, one launch (start us, length us, event | category | flops | bytes accessed | tf_op | source)
XLA Modules:
  0.0 609.0 jit_solution(10747280087941520110)
XLA Ops:
  9.2 6.4 %all-to-all-start.1 = ((s32[8,1,192]{2,1,0:T(1,128)}), s32[8,1,192]{2,1,0:T(1,128)S(1)}, u32[]{:S(2)}, u32[]{:S(2)}) async-start(s32[8,1,192]{2,1,0:T(1,128)} %broadcast_in_dim.36), calls=%async_computation.1 | async-start | bytes 16384 | tf_op jit(solution)/shard_map/all_to_all | solution.py:25
  15.6 2.1 copy.118
  17.7 3.5 all-to-all-done.1
  21.2 3.6 all-to-all-start
  25.7 19.9 %all-to-all-done = bf16[192,8,256]{2,0,1:T(8,128)(2,1)S(1)} async-done(((bf16[192,8,256]{2,0,1:T(8,128)(2,1)}), bf16[192,8,256]{2,0,1:T(8,128)(2,1)S(1)}, u32[]{:S(2)}, u32[]{:S(2)}) %all-to-all-start) | async-done | bytes 786464 | tf_op jit(solution)/shard_map/all_to_all | solution.py:18
  45.6 3.5 all-to-all-start.2
  50.1 19.9 %all-to-all-done.2 = bf16[192,8,256]{2,0,1:T(8,128)(2,1)S(1)} async-done(((bf16[192,8,256]{2,0,1:T(8,128)(2,1)}), bf16[192,8,256]{2,0,1:T(8,128)(2,1)S(1)}, u32[]{:S(2)}, u32[]{:S(2)}) %all-to-all-start.2) | async-done | bytes 786464 | tf_op jit(solution)/shard_map/all_to_all | solution.py:19
  70.1 3.5 all-to-all-start.4
  73.6 26.4 %all-gather.5.cloned.1.call-done = bf16[2048,2048]{1,0:T(8,128)(2,1)} async-done(((bf16[512,2048]{1,0:T(8,128)(2,1)}), bf16[2048,2048]{1,0:T(8,128)(2,1)}) %all-gather.5.cloned.1.call-update) | async-done | bytes 8388624 | tf_op jit(solution)/shard_map/all_gather | solution.py:13
  100.1 6.3 %convolution_convert_fusion.1 = bf16[192,2048]{1,0:T(8,128)(2,1)S(1)} fusion(bf16[192,2048]{1,0:T(8,128)(2,1)S(1)} %copy-done.7, bf16[2048,2048]{1,0:T(8,128)(2,1)} %all-gather.5.cloned.1.call-done), kind=kOutput, calls=%fused_computation.31 | convolution fusion | flops 1611005952 | bytes 9961472 | tf_op jit(solution)/shard_map/dot_general | solution.py:11
  107.3 4.6 all-to-all-start.3
  113.0 2.7 reshape.124
  115.7 2.7 reshape.127
  118.4 2.1 copy.66
  120.5 2.7 reshape.129
  123.3 3.1 copy.68
  126.3 6.6 %all-to-all-done.3 = bf16[192,8,256]{2,0,1:T(8,128)(2,1)} async-done(((bf16[192,8,256]{2,0,1:T(8,128)(2,1)}), bf16[192,8,256]{2,0,1:T(8,128)(2,1)}, u32[]{:S(2)}, u32[]{:S(2)}) %all-to-all-start.3) | async-done | bytes 786464 | tf_op jit(solution)/shard_map/all_to_all | solution.py:22
  133.0 2.7 reshape.128
  135.7 63.9 %while.17 = (s32[]{:T(128)}, f32[1536,2,128]{0,2,1:T(8,128)S(1)}, f32[1536,2,128]{0,2,1:T(8,128)S(1)}, bf16[3,512,2,128]{3,2,1,0:T(2,128)(2,1)}, bf16[3,512,2,12...) while((s32[]{:T(128)}, f32[1536,2,128]{0,2,1:T(8,128)S(1)}, ...), condition=%wide.region_4.5_spmd.clone, body=%wide.region_0.4_spmd.clone.sunk | while | flops 2435711488 | bytes 78939944 | solution.py:79
  135.7 1.8 constant_dynamic-slice_fusion.6
  137.5 1.1 constant_dynamic-slice_fusion.8
  138.7 1.5 compare_or_fusion.2
  140.1 6.4 %fusion.54 = (f32[2,512]{1,0:T(2,128)S(1)}, f32[2,512,1536]{2,1,0:T(8,128)}) fusion(pred[512,1536]{1,0:T(8,128)(4,1)} %compare_or_fusion.2, bf16[1536,2,128]{2,0,1:T(8,128)(2,1)} %get-tuple-element.300, bf16[1,512,2,128]{3,2,1,0:T(2,128)(2,1)S(1)} %constant_dynamic-slice_fusion.8), kind=kOutput, calls=%fused_computation.53.clone.1 | convolution fusion | flops 408946176 | bytes 8130560 | tf_op jit(solution)/shard_map/while/body/eval_jaxpr/sub | solution.py:50
  146.5 3.8 fusion.55
  150.3 1.1 multiply_reduce_fusion.2
  152.4 1.2 multiply_convert_fusion.3
  155.7 1.3 copy_dynamic-update-slice_fusion.3
  157.0 1.8 constant_dynamic-slice_fusion.6
  158.8 1.1 constant_dynamic-slice_fusion.8
  160.0 1.5 compare_or_fusion.2
  161.4 6.4 %fusion.54 = (f32[2,512]{1,0:T(2,128)S(1)}, f32[2,512,1536]{2,1,0:T(8,128)}) fusion(pred[512,1536]{1,0:T(8,128)(4,1)} %compare_or_fusion.2, bf16[1536,2,128]{2,0,1:T(8,128)(2,1)} %get-tuple-element.300, bf16[1,512,2,128]{3,2,1,0:T(2,128)(2,1)S(1)} %constant_dynamic-slice_fusion.8), kind=kOutput, calls=%fused_computation.53.clone.1 | convolution fusion | flops 408946176 | bytes 8130560 | tf_op jit(solution)/shard_map/while/body/eval_jaxpr/sub | solution.py:50
  167.8 3.8 fusion.55
  171.6 1.1 multiply_reduce_fusion.2
  173.7 1.2 multiply_convert_fusion.3
  176.9 1.3 copy_dynamic-update-slice_fusion.3
  178.3 1.8 constant_dynamic-slice_fusion.6
  180.1 1.1 constant_dynamic-slice_fusion.8
  181.3 1.5 compare_or_fusion.2
  182.7 6.4 %fusion.54 = (f32[2,512]{1,0:T(2,128)S(1)}, f32[2,512,1536]{2,1,0:T(8,128)}) fusion(pred[512,1536]{1,0:T(8,128)(4,1)} %compare_or_fusion.2, bf16[1536,2,128]{2,0,1:T(8,128)(2,1)} %get-tuple-element.300, bf16[1,512,2,128]{3,2,1,0:T(2,128)(2,1)S(1)} %constant_dynamic-slice_fusion.8), kind=kOutput, calls=%fused_computation.53.clone.1 | convolution fusion | flops 408946176 | bytes 8130560 | tf_op jit(solution)/shard_map/while/body/eval_jaxpr/sub | solution.py:50
  189.1 3.8 fusion.55
  195.0 1.2 multiply_convert_fusion.3
  198.2 1.3 copy_dynamic-update-slice_fusion.3
  199.6 3.1 all_to_all.145
  202.7 24.4 %all_to_all.162 = bf16[8,192,256]{2,1,0:T(8,128)(2,1)S(1)} all-to-all(bf16[8,192,256]{2,1,0:T(8,128)(2,1)} %all_to_all.145), channel_id=1, replica_groups=mesh['dp'=4,'seq'=8] {'seq'}, dimensions={0} | all-to-all | bytes 1572864 | tf_op jit(solution)/shard_map/all_to_all | solution.py:87
  227.1 1.3 copy.76
  228.4 2.6 all_to_all.148
  231.1 2.2 copy.77
  233.2 4.2 all-to-all-start.9
  237.7 10.5 %all-to-all-done.9 = bf16[192,4,512]{2,0,1:T(8,128)(2,1)} async-done(((bf16[192,4,512]{2,0,1:T(8,128)(2,1)}), bf16[192,4,512]{2,0,1:T(8,128)(2,1)}, u32[]{:S(2)}, u32[]{:S(2)}) %all-to-all-start.9) | async-done | bytes 786464 | tf_op jit(solution)/shard_map/all_to_all | solution.py:92
  248.2 6.0 fusion.20
  254.2 3.1 all_to_all.133
  257.4 4.2 all-to-all-start.5
  262.6 2.3 copy.71
  265.0 1.4 all_to_all.137
  266.3 33.5 %all-to-all-done.5 = bf16[8,192,256]{2,1,0:T(8,128)(2,1)} async-done(((bf16[8,192,256]{2,1,0:T(8,128)(2,1)}), bf16[8,192,256]{2,1,0:T(8,128)(2,1)}, u32[]{:S(2)}, u32[]{:S(2)}) %all-to-all-start.5) | async-done | bytes 786464 | tf_op jit(solution)/shard_map/all_to_all | solution.py:88
  299.8 15.5 %all-to-all-start.6 = ((bf16[8,192,256]{2,1,0:T(8,128)(2,1)}), bf16[8,192,256]{2,1,0:T(8,128)(2,1)S(1)}, u32[]{:S(2)}, u32[]{:S(2)}) async-start(bf16[8,192,256]{2,1,0:T(8,128)(2,1)} %all_to_all.137), calls=%async_computation.6 | async-start | bytes 1572864 | tf_op jit(solution)/shard_map/all_to_all | solution.py:89
  316.3 2.3 copy.73
  318.6 1.4 all_to_all.141
  319.9 36.4 %all-to-all-done.6 = bf16[8,192,256]{2,1,0:T(8,128)(2,1)S(1)} async-done(((bf16[8,192,256]{2,1,0:T(8,128)(2,1)}), bf16[8,192,256]{2,1,0:T(8,128)(2,1)S(1)}, u32[]{:S(2)}, u32[]{:S(2)}) %all-to-all-start.6) | async-done | bytes 786464 | tf_op jit(solution)/shard_map/all_to_all | solution.py:89
  356.3 3.5 all-to-all-start.7
  359.9 2.1 copy.92
  363.0 44.3 %all-to-all-done.7 = bf16[8,192,256]{2,1,0:T(8,128)(2,1)S(1)} async-done(((bf16[8,192,256]{2,1,0:T(8,128)(2,1)}), bf16[8,192,256]{2,1,0:T(8,128)(2,1)S(1)}, u32[]{:S(2)}, u32[]{:S(2)}) %all-to-all-start.7) | async-done | bytes 786464 | tf_op jit(solution)/shard_map/all_to_all | solution.py:90
  408.3 180.0 %all-gather.9.cloned.1.call-done = f32[4096,2048]{1,0:T(8,128)} async-done(((f32[512,2048]{1,0:T(8,128)}), f32[4096,2048]{1,0:T(8,128)}) %all-gather.9.cloned.1.call-update) | async-done | bytes 33554448 | tf_op jit(solution)/shard_map/all_gather | solution.py:94
  588.3 14.1 %reduce_sum.27 = f32[512,2048]{1,0:T(8,128)} reduce(f32[8,512,2048]{2,1,0:T(8,128)} %bitcast.122, f32[]{:T(128)} %constant.42.clone.1), dimensions={0}, to_apply=%region_5.6 | reduce | flops 7340032 | bytes 37748740 | tf_op jit(solution)/shard_map/reduce_sum | solution.py:93
  (85 shorter events, 19.9 us)
Async XLA Ops:
  7.2 17.6 %copy-start.5 = (bf16[192,2048]{1,0:T(8,128)(2,1)S(1)}, bf16[192,2048]{1,0:T(8,128)(2,1)}, u32[]{:S(2)}) copy-start(bf16[192,2048]{1,0:T(8,128)(2,1)} %param.10) | copy-start | bytes 2359300
  7.2 92.9 %all-gather.5.cloned.1.call-start = ((), (), s32[]{:S(2)}) async-start(), calls=%async_computation.10 | async-start | bytes 10485760 | tf_op jit(solution)/shard_map/all_gather | solution.py:13
  9.2 12.0 %all-to-all-start.1 = ((s32[8,1,192]{2,1,0:T(1,128)}), s32[8,1,192]{2,1,0:T(1,128)S(1)}, u32[]{:S(2)}, u32[]{:S(2)}) async-start(s32[8,1,192]{2,1,0:T(1,128)} %broadcast_in_dim.36), calls=%async_computation.1 | async-start | bytes 16384 | tf_op jit(solution)/shard_map/all_to_all | solution.py:25
  15.6 33.6 %copy-start.6 = (bf16[192,2048]{1,0:T(8,128)(2,1)S(1)}, bf16[192,2048]{1,0:T(8,128)(2,1)}, u32[]{:S(2)}) copy-start(bf16[192,2048]{1,0:T(8,128)(2,1)} %param.11) | copy-start | bytes 2359300
  21.2 24.5 %all-to-all-start = ((bf16[192,8,256]{2,0,1:T(8,128)(2,1)}), bf16[192,8,256]{2,0,1:T(8,128)(2,1)S(1)}, u32[]{:S(2)}, u32[]{:S(2)}) async-start(bf16[192,8,256]{2,0,1:T(8,128)(2,1)} %bitcast.79), calls=%async_computation | async-start | bytes 1572864 | tf_op jit(solution)/shard_map/all_to_all | solution.py:18
  24.8 75.3 %copy-start.7 = (bf16[192,2048]{1,0:T(8,128)(2,1)S(1)}, bf16[192,2048]{1,0:T(8,128)(2,1)}, u32[]{:S(2)}) copy-start(bf16[192,2048]{1,0:T(8,128)(2,1)} %param.12) | copy-start | bytes 2359300
  45.6 60.7 %copy-start.2 = (bf16[192,8,256]{2,0,1:T(8,128)(2,1)}, bf16[192,8,256]{2,0,1:T(8,128)(2,1)S(1)}, u32[]{:S(2)}) copy-start(bf16[192,8,256]{2,0,1:T(8,128)(2,1)S(1)} %all-to-all-done) | copy-start | bytes 2359300
  45.6 24.4 %all-to-all-start.2 = ((bf16[192,8,256]{2,0,1:T(8,128)(2,1)}), bf16[192,8,256]{2,0,1:T(8,128)(2,1)S(1)}, u32[]{:S(2)}, u32[]{:S(2)}) async-start(bf16[192,8,256]{2,0,1:T(8,128)(2,1)} %bitcast.78), calls=%async_computation.2 | async-start | bytes 1572864 | tf_op jit(solution)/shard_map/all_to_all | solution.py:19
  70.1 36.3 %copy-start.3 = (bf16[192,8,256]{2,0,1:T(8,128)(2,1)}, bf16[192,8,256]{2,0,1:T(8,128)(2,1)S(1)}, u32[]{:S(2)}) copy-start(bf16[192,8,256]{2,0,1:T(8,128)(2,1)S(1)} %all-to-all-done.2) | copy-start | bytes 2359300
  70.1 37.3 %all-to-all-start.4 = ((bf16[192,8,256]{2,0,1:T(8,128)(2,1)}), bf16[192,8,256]{2,0,1:T(8,128)(2,1)S(1)}, u32[]{:S(2)}, u32[]{:S(2)}) async-start(bf16[192,8,256]{2,0,1:T(8,128)(2,1)} %bitcast.76), calls=%async_computation.4 | async-start | bytes 1572864 | tf_op jit(solution)/shard_map/all_to_all | solution.py:20
  107.3 5.4 copy-start.4
  107.3 25.7 %all-to-all-start.3 = ((bf16[192,8,256]{2,0,1:T(8,128)(2,1)}), bf16[192,8,256]{2,0,1:T(8,128)(2,1)}, u32[]{:S(2)}, u32[]{:S(2)}) async-start(bf16[192,8,256]{2,0,1:T(8,128)(2,1)} %bitcast.77), calls=%async_computation.3 | async-start | bytes 1572864 | tf_op jit(solution)/shard_map/all_to_all | solution.py:22
  111.9 125.8 %all-gather.7.cloned.1.call-start = ((), (), s32[]{:S(2)}) async-start(), calls=%async_computation.11 | async-start | bytes 3932160 | tf_op jit(solution)/shard_map/all_gather | solution.py:30
  146.5 3.8 copy-start.1
  146.5 3.8 copy-start.8
  146.5 5.9 slice-start
  150.3 2.1 slice-start.1
  152.4 1.3 copy-start
  167.8 3.8 copy-start.1
  167.8 3.8 copy-start.8
  167.8 5.9 slice-start
  171.6 2.1 slice-start.1
  173.7 1.3 copy-start
  189.1 3.8 copy-start.1
  189.1 3.8 copy-start.8
  189.1 5.9 slice-start
  192.9 2.1 slice-start.1
  195.0 1.3 copy-start
  233.2 15.0 %all-to-all-start.9 = ((bf16[192,4,512]{2,0,1:T(8,128)(2,1)}), bf16[192,4,512]{2,0,1:T(8,128)(2,1)}, u32[]{:S(2)}, u32[]{:S(2)}) async-start(bf16[192,4,512]{2,0,1:T(8,128)(2,1)} %copy.77), calls=%async_computation.9 | async-start | bytes 1572864 | tf_op jit(solution)/shard_map/all_to_all | solution.py:92
  237.4 350.9 %all-gather.9.cloned.1.call-start = ((), (), s32[]{:S(2)}) async-start(), calls=%async_computation.12 | async-start | bytes 37748736 | tf_op jit(solution)/shard_map/all_gather | solution.py:94
  257.4 42.5 %all-to-all-start.5 = ((bf16[8,192,256]{2,1,0:T(8,128)(2,1)}), bf16[8,192,256]{2,1,0:T(8,128)(2,1)}, u32[]{:S(2)}, u32[]{:S(2)}) async-start(bf16[8,192,256]{2,1,0:T(8,128)(2,1)} %all_to_all.133), calls=%async_computation.5 | async-start | bytes 1572864 | tf_op jit(solution)/shard_map/all_to_all | solution.py:88
  299.8 56.5 %all-to-all-start.6 = ((bf16[8,192,256]{2,1,0:T(8,128)(2,1)}), bf16[8,192,256]{2,1,0:T(8,128)(2,1)S(1)}, u32[]{:S(2)}, u32[]{:S(2)}) async-start(bf16[8,192,256]{2,1,0:T(8,128)(2,1)} %all_to_all.137), calls=%async_computation.6 | async-start | bytes 1572864 | tf_op jit(solution)/shard_map/all_to_all | solution.py:89
  356.3 51.0 %all-to-all-start.7 = ((bf16[8,192,256]{2,1,0:T(8,128)(2,1)}), bf16[8,192,256]{2,1,0:T(8,128)(2,1)S(1)}, u32[]{:S(2)}, u32[]{:S(2)}) async-start(bf16[8,192,256]{2,1,0:T(8,128)(2,1)} %all_to_all.141), calls=%async_computation.7 | async-start | bytes 1572864 | tf_op jit(solution)/shard_map/all_to_all | solution.py:90
Sparse Core Ops, SparseCore 0:
  9.8 90.1 all-gather.4
  114.6 44.3 all-gather.6
  254.3 333.9 all-gather.8
